TPU v7x, 32 devices: a whole 2x2x4 slice. The times are simulated.
32 devices in a mesh: groups: 2 (over y), space: 8 (over z, core), member: 2 (over x).
Axes of the slice: x: 2, y: 2, z: 4, core: 2. Of those that a mesh axis runs over, the one named last changes fastest.
Arguments:
- features: bfloat16 [4, 256, 128, 256], P(('groups', 'member'), None, 'space'), parts along dimension 0, may hold values from -6 to 6
- views: int32 [4], P('groups'), parts along dimension 0, may hold values from 8 to 29
- conv_first: bfloat16 [3, 3, 256, 256], replicated, may hold values from -0.125 to 0.125
- bias_first: float32 [256], replicated, may hold values from -3 to 3
- conv_second: bfloat16 [3, 3, 256, 256], replicated, may hold values from -0.125 to 0.125
- bias_second: float32 [256], replicated, may hold values from -3 to 3
- classify: bfloat16 [19, 256], replicated, may hold values from -0.375 to 0.375
- class_bias: float32 [19], replicated, may hold values from -3 to 3
Outputs:
- ensemble_logits: float32 [1024, 19, 1024], P(('groups', 'space', 'member')), parts along dimension 0
There are 2 independent parts, one for each index of `groups`. A program takes and returns all parts, laid end to end along the dimension named above; an argument that names none is the same for every part. Nothing has to cross between parts.
All inputs are finite; a program needn't handle non-finite values.
Results may differ from a plain program's by a relative error of at most 0.0035.
Values may be sent and summed in bfloat16 or wider, within the bound.
No kernel may reach another device: no remote copies, remote signals or barrier semaphores. Data moves between devices by JAX's collectives and lax.ppermute only.
A program may use at most 128 MiB of HBM per device.

v0:
```python
import jax
import jax.numpy as jnp
from jax import lax
from jax.sharding import PartitionSpec as P

UP = 4


def with_halo(block, sides, width):
    for axis, dim in sides:
        count = lax.axis_size(axis)
        forward = [(i, i + 1) for i in range(count - 1)]
        backward = [(target, source) for source, target in forward]
        low = lax.ppermute(
            lax.slice_in_dim(block, block.shape[dim] - width, None, axis=dim), axis, forward
        )
        high = lax.ppermute(lax.slice_in_dim(block, 0, width, axis=dim), axis, backward)
        block = jnp.concatenate([low, block, high], axis=dim)
    return block


def resize_matrix(positions, out_len, valid, in_len):
    numer = (2 * positions + 1) * valid - out_len
    denom = 2 * out_len
    lower = numer // denom
    frac = (numer - lower * denom).astype(jnp.float32) / denom
    below = numer < 0
    frac = jnp.where(below, jnp.float32(0.0), frac)
    lower = jnp.where(below, 0, lower)
    top_index = valid - 1
    over = lower >= top_index
    frac = jnp.where(over, jnp.float32(0.0), frac)
    lower = jnp.where(over, top_index, lower)
    columns = jnp.arange(in_len, dtype=jnp.int32)
    first = jnp.where(columns[None, :] == lower[:, None], 1.0 - frac[:, None], jnp.float32(0.0))
    second = jnp.where(columns[None, :] == lower[:, None] + 1, frac[:, None], jnp.float32(0.0))
    return (first + second).astype(jnp.bfloat16)


def convolve(field, weights):
    height, width = (field.shape[1], field.shape[2])
    padded = with_halo(field, (("space", 1),), 1)
    padded = jnp.pad(padded, ((0, 0), (0, 0), (1, 1)))
    total = jnp.zeros((weights.shape[2], height, width), jnp.float32)
    for row_tap in range(3):
        for col_tap in range(3):
            window = padded[:, row_tap : row_tap + height, col_tap : col_tap + width]
            total = total + jnp.einsum(
                "oc,cyx->oyx", weights[row_tap, col_tap], window, preferred_element_type=jnp.float32
            )
    return total


def window_start(numer, first_row, full_rows, out_rows, window_rows):
    valid = full_rows * numer // 14
    numer_pos = (2 * first_row + 1) * valid - out_rows
    lower = numer_pos // (2 * out_rows)
    lower = jnp.where(numer_pos < 0, 0, lower)
    lower = jnp.where(lower >= valid - 1, valid - 1, lower)
    return jnp.clip(lower, 0, full_rows - window_rows)


def column_table(numer, flip, cols, out_cols):
    valid_cols = cols * numer // 14
    col_pos = jnp.arange(out_cols, dtype=jnp.int32)
    col_pos = jnp.where(flip == 1, out_cols - 1 - col_pos, col_pos)
    return resize_matrix(col_pos, out_cols, valid_cols, cols)


def shards(features, views, conv_first, bias_first, conv_second, bias_second, classify, class_bias):
    feat = features[0]
    rows_dev, cols = (feat.shape[1], feat.shape[2])
    spaces = lax.axis_size("space")
    full_rows = rows_dev * spaces
    place = lax.axis_index("space")
    member_index = lax.axis_index("member")
    members = views.shape[0]
    picked = jnp.arange(members, dtype=jnp.int32) == member_index
    code = jnp.sum(jnp.where(picked, views, 0))
    numer = code // 2
    valid_rows = full_rows * numer // 14
    valid_cols = cols * numer // 14
    row_ids = place * rows_dev + jnp.arange(rows_dev, dtype=jnp.int32)
    row_ok = row_ids < valid_rows
    col_ok = jnp.arange(cols, dtype=jnp.int32) < valid_cols
    mask = (row_ok[:, None] & col_ok[None, :]).astype(jnp.float32)
    first = feat * mask.astype(jnp.bfloat16)
    hidden = (jax.nn.relu(convolve(first, conv_first) + bias_first[:, None, None]) * mask).astype(
        jnp.bfloat16
    )
    second = (
        jax.nn.relu(convolve(hidden, conv_second) + bias_second[:, None, None]) * mask
    ).astype(jnp.bfloat16)
    logits = (
        jnp.einsum("kc,cyx->kyx", classify, second, preferred_element_type=jnp.float32)
        + class_bias[:, None, None]
    ).astype(jnp.bfloat16)
    out_rows = UP * full_rows
    out_cols = UP * cols
    own_rows = out_rows // spaces
    part_rows = own_rows // members
    window_rows = (part_rows - 1) // UP + 3
    gathered = lax.all_gather(logits, "space", axis=1, tiled=True)
    pieces = []
    for target in range(members):
        first_row = place * own_rows + target * part_rows
        begin = window_start(numer, first_row, full_rows, out_rows, window_rows)
        pieces.append(lax.dynamic_slice_in_dim(gathered, begin, window_rows, 1))
    outgoing = jnp.stack(pieces, 0)
    incoming = lax.all_to_all(outgoing, "member", split_axis=0, concat_axis=0, tiled=True)
    own_first = place * own_rows + member_index * part_rows
    positions = own_first + jnp.arange(part_rows, dtype=jnp.int32)
    result = jnp.zeros((part_rows, logits.shape[0], out_cols), jnp.float32)
    for source in range(members):
        source_numer = views[source] // 2
        source_flip = views[source] % 2
        source_valid = full_rows * source_numer // 14
        begin = window_start(source_numer, own_first, full_rows, out_rows, window_rows)
        source_cols = column_table(source_numer, source_flip, cols, out_cols)
        row_table = resize_matrix(positions, out_rows, source_valid, full_rows)
        row_part = lax.dynamic_slice_in_dim(row_table, begin, window_rows, 1)
        widened = jnp.einsum(
            "cyx,jx->cyj", incoming[source], source_cols, preferred_element_type=jnp.float32
        ).astype(jnp.bfloat16)
        result = result + jnp.einsum(
            "iy,cyj->icj", row_part, widened, preferred_element_type=jnp.float32
        )
    return result


def solution(mesh):
    placed = (
        P(("groups", "member"), None, "space", None),
        P("groups"),
        P(),
        P(),
        P(),
        P(),
        P(),
        P(),
    )
    return jax.shard_map(
        shards,
        mesh=mesh,
        in_specs=placed,
        out_specs=P(("groups", "space", "member"), None, None),
        check_vma=False,
    )
```

profile of v0, /device:TPU:0, one launch (start us, length us, event | category | flops | bytes accessed | tf_op | source)
XLA Modules:
  0.0 144.4 jit_solution(15678336219757409563)
XLA Ops:
  6.5 0.0 all-gather.2.cloned.1.call-start
  6.5 1.3 fusion.170
  10.5 4.3 %copy.22 = bf16[1,256,16,256]{1,3,2,0:T(8,128)(2,1)} copy(bf16[1,256,16,256]{3,2,1,0:T(8,128)(2,1)} %param.8) | data formatting | bytes 4194304 | tf_op args[0]
  14.8 0.1 fusion.147
  14.9 2.1 %bitcast_multiply_fusion = bf16[256,16,256]{0,2,1:T(8,128)(2,1)S(1)} fusion(bf16[1,256,16,256]{1,3,2,0:T(8,128)(2,1)} %copy.22, bf16[16,256]{1,0:T(8,128)(2,1)S(1)} %get-tuple-element.21), kind=kLoop, calls=%fused_computation.54 | loop fusion | flops 1048576 | bytes 4202496 | tf_op jit(solution)/shard_map/mul | solution.py:87
  16.9 0.0 copy-start.2
  17.0 2.5 %collective-permute-start = (bf16[256,1,256]{0,2,1:T(8,128)(2,1)S(1)}, bf16[256,1,256]{0,2,1:T(8,128)(2,1)S(1)}, u32[]{:S(2)}, u32[]{:S(2)}) collective-permute-start(bf16[256,1,256]{0,2,1:T(8,128)(2,1)S(1)} %get-tuple-element.15), channel_id=1, source_target_pairs={{0,2},{2,4},{4,6},{6,8},{8,10},{10,12},{12,14},{1,3},{3,5},{5,7},{... | collective-permute-start | bytes 393224 | tf_op jit(solution)/shard_map/ppermute | solution.py:14
  19.5 1.3 collective-permute-start.1
  20.8 0.1 multiply_bitcast_fusion
  20.9 0.0 copy-done.2
  20.9 1.7 %fusion.52 = f32[16,256,256]{2,1,0:T(8,128)S(1)} fusion(bf16[256,16,256]{2,1,0:T(8,128)(2,1)S(1)} %multiply_bitcast_fusion, bf16[3,3,256,256]{3,2,1,0:T(8,128)(2,1)S(1)} %copy-done.2), kind=kOutput, calls=%fused_computation.55 | convolution fusion | flops 536870912 | bytes 6422528 | tf_op jit(solution)/shard_map/oc,cyx->oyx/dot_general | solution.py:48
  22.6 0.0 collective-permute-done
  22.6 2.3 %collective-permute-done.1 = bf16[256,1,256]{0,2,1:T(8,128)(2,1)S(1)} collective-permute-done((bf16[256,1,256]{0,2,1:T(8,128)(2,1)S(1)}, bf16[256,1,256]{0,2,1:T(8,128)(2,1)S(1)}, u32[]{:S(2)}, u32[]{:S(2)}) %collective-permute-start.1) | collective-permute-done | bytes 131104 | tf_op jit(solution)/shard_map/ppermute | solution.py:17
  24.9 0.8 fusion.5
  25.8 0.7 fusion.40
  26.5 2.8 %fusion.42 = f32[16,256,256]{2,1,0:T(8,128)} fusion(bf16[256,18,258]{0,2,1:T(8,128)(2,1)S(1)} %fusion.5, bf16[3,3,256,256]{3,2,1,0:T(8,128)(2,1)S(1)} %copy-done.2), kind=kOutput, calls=%fused_computation.44 | convolution fusion | flops 536870912 | bytes 6422528 | tf_op jit(solution)/shard_map/oc,cyx->oyx/dot_general | solution.py:48
  29.3 2.7 %fusion.44 = f32[16,256,256]{2,1,0:T(8,128)} fusion(bf16[256,18,258]{0,2,1:T(8,128)(2,1)S(1)} %fusion.5, bf16[3,3,256,256]{3,2,1,0:T(8,128)(2,1)S(1)} %copy-done.2), kind=kOutput, calls=%fused_computation.46 | convolution fusion | flops 536870912 | bytes 6422528 | tf_op jit(solution)/shard_map/oc,cyx->oyx/dot_general | solution.py:48
  32.0 2.7 %fusion.46 = f32[16,256,256]{2,1,0:T(8,128)} fusion(bf16[256,18,258]{0,2,1:T(8,128)(2,1)S(1)} %fusion.5, bf16[3,3,256,256]{3,2,1,0:T(8,128)(2,1)S(1)} %copy-done.2), kind=kOutput, calls=%fused_computation.48 | convolution fusion | flops 536870912 | bytes 6422528 | tf_op jit(solution)/shard_map/oc,cyx->oyx/dot_general | solution.py:48
  34.7 2.7 %fusion.48 = f32[16,256,256]{2,1,0:T(8,128)} fusion(bf16[256,18,258]{0,2,1:T(8,128)(2,1)S(1)} %fusion.5, bf16[3,3,256,256]{3,2,1,0:T(8,128)(2,1)S(1)} %copy-done.2), kind=kOutput, calls=%fused_computation.50 | convolution fusion | flops 536870912 | bytes 6422528 | tf_op jit(solution)/shard_map/oc,cyx->oyx/dot_general | solution.py:48
  37.4 2.8 %fusion.6 = f32[16,256,256]{2,1,0:T(8,128)} fusion(bf16[256,16,256]{0,2,1:T(8,128)(2,1)S(1)} %bitcast_multiply_fusion, bf16[256,1,256]{0,2,1:T(8,128)(2,1)S(1)} %collective-permute-done, bf16[3,3,256,256]{3,2,1,0:T(8,128)(2,1)S(1)} %copy-done.2), kind=kOutput, calls=%fused_computation.12 | convolution fusion | flops 541327360 | bytes 6553600 | tf_op jit(solution)/shard_map/oc,cyx->oyx/dot_general | solution.py:48
  40.2 2.7 %fusion.10 = f32[16,256,256]{2,1,0:T(8,128)} fusion(bf16[256,1,256]{0,2,1:T(8,128)(2,1)S(1)} %collective-permute-done.1, bf16[256,16,256]{0,2,1:T(8,128)(2,1)S(1)} %bitcast_multiply_fusion, bf16[3,3,256,256]{3,2,1,0:T(8,128)(2,1)S(1)} %copy-done.2), kind=kOutput, calls=%fused_computation.16 | convolution fusion | flops 541327360 | bytes 6553600 | tf_op jit(solution)/shard_map/oc,cyx->oyx/dot_general | solution.py:48
  42.8 9.7 %fusion.54 = bf16[256,16,256]{0,2,1:T(8,128)(2,1)S(1)} fusion(f32[16,256]{1,0:T(8,128)S(1)} %get-tuple-element.22, f32[256]{0:T(256)S(1)} %copy-done.5, bf16[256,18,258]{0,2,1:T(8,128)(2,1)S(1)} %fusion.5, f32[16,256,256]{2,1,0:T(8,128)} %fusion.10, f32[16,256,256]{2,1,0:T(8,128)S(1)} %fusion.40, f32[16,256,256]{2,1,0:T(8,128)} %fusion.42, ...), kind=kOutput, calls=%fused_computation.59 | convolution fusion | flops 549453824 | bytes 37897216 | tf_op jit(solution)/shard_map/oc,cyx->oyx/dot_general | solution.py:48
  52.6 5.4 %collective-permute-start.2 = (bf16[256,1,256]{0,2,1:T(8,128)(2,1)S(1)}, bf16[256,1,256]{0,2,1:T(8,128)(2,1)S(1)}, u32[]{:S(2)}, u32[]{:S(2)}) collective-permute-start(bf16[256,1,256]{0,2,1:T(8,128)(2,1)S(1)} %get-tuple-element.13), channel_id=1, source_target_pairs={{0,2},{2,4},{4,6},{6,8},{8,10},{10,12},{12,14},{1,3},{3,5},{5,7},{... | collective-permute-start | bytes 393224 | tf_op jit(solution)/shard_map/ppermute | solution.py:14
  58.1 1.5 %collective-permute-start.3 = (bf16[256,1,256]{0,2,1:T(8,128)(2,1)S(1)}, bf16[256,1,256]{0,2,1:T(8,128)(2,1)S(1)}, u32[]{:S(2)}, u32[]{:S(2)}) collective-permute-start(bf16[256,1,256]{0,2,1:T(8,128)(2,1)S(1)} %get-tuple-element.14), channel_id=1, source_target_pairs={{2,0},{4,2},{6,4},{8,6},{10,8},{12,10},{14,12},{3,1},{5,3},{7,5},{... | collective-permute-start | bytes 393224 | tf_op jit(solution)/shard_map/ppermute | solution.py:17
  59.5 3.6 %fusion.108 = f32[16,256,256]{2,1,0:T(8,128)} fusion(bf16[256,16,256]{0,2,1:T(8,128)(2,1)S(1)} %fusion.54, bf16[3,3,256,256]{3,2,1,0:T(8,128)(2,1)} %param.12), kind=kOutput, calls=%fused_computation.91 | convolution fusion | flops 536870912 | bytes 6422528 | tf_op jit(solution)/shard_map/oc,cyx->oyx/dot_general | solution.py:48
  63.1 0.0 collective-permute-done.2
  63.1 0.0 collective-permute-done.3
  63.1 0.9 select_maximum_fusion
  64.0 0.4 copy-done.3
  64.4 2.8 %fusion.26 = f32[16,256,256]{2,1,0:T(8,128)} fusion(bf16[256,18,258]{0,2,1:T(8,128)(2,1)S(1)} %select_maximum_fusion, bf16[3,3,256,256]{3,2,1,0:T(8,128)(2,1)S(1)} %copy-done.3), kind=kOutput, calls=%fused_computation.30 | convolution fusion | flops 536870912 | bytes 6422528 | tf_op jit(solution)/shard_map/oc,cyx->oyx/dot_general | solution.py:48
  67.2 2.7 %fusion.28 = f32[16,256,256]{2,1,0:T(8,128)} fusion(bf16[256,18,258]{0,2,1:T(8,128)(2,1)S(1)} %select_maximum_fusion, bf16[3,3,256,256]{3,2,1,0:T(8,128)(2,1)S(1)} %copy-done.3), kind=kOutput, calls=%fused_computation.32 | convolution fusion | flops 536870912 | bytes 6422528 | tf_op jit(solution)/shard_map/oc,cyx->oyx/dot_general | solution.py:48
  69.9 2.7 %fusion.30 = f32[16,256,256]{2,1,0:T(8,128)} fusion(bf16[256,18,258]{0,2,1:T(8,128)(2,1)S(1)} %select_maximum_fusion, bf16[3,3,256,256]{3,2,1,0:T(8,128)(2,1)S(1)} %copy-done.3), kind=kOutput, calls=%fused_computation.34 | convolution fusion | flops 536870912 | bytes 6422528 | tf_op jit(solution)/shard_map/oc,cyx->oyx/dot_general | solution.py:48
  72.6 2.8 %fusion.32 = f32[16,256,256]{2,1,0:T(8,128)} fusion(bf16[256,18,258]{0,2,1:T(8,128)(2,1)S(1)} %select_maximum_fusion, bf16[3,3,256,256]{3,2,1,0:T(8,128)(2,1)S(1)} %copy-done.3), kind=kOutput, calls=%fused_computation.36 | convolution fusion | flops 536870912 | bytes 6422528 | tf_op jit(solution)/shard_map/oc,cyx->oyx/dot_general | solution.py:48
  75.4 2.7 %fusion.34 = f32[16,256,256]{2,1,0:T(8,128)} fusion(bf16[256,18,258]{0,2,1:T(8,128)(2,1)S(1)} %select_maximum_fusion, bf16[3,3,256,256]{3,2,1,0:T(8,128)(2,1)S(1)} %copy-done.3), kind=kOutput, calls=%fused_computation.38 | convolution fusion | flops 536870912 | bytes 6422528 | tf_op jit(solution)/shard_map/oc,cyx->oyx/dot_general | solution.py:48
  78.1 2.7 %fusion.14 = f32[16,256,256]{2,1,0:T(8,128)} fusion(bf16[256,16,256]{0,2,1:T(8,128)(2,1)S(1)} %fusion.54, bf16[256,1,256]{0,2,1:T(8,128)(2,1)S(1)} %collective-permute-done.2, bf16[3,3,256,256]{3,2,1,0:T(8,128)(2,1)S(1)} %copy-done.3), kind=kOutput, calls=%fused_computation.20 | convolution fusion | flops 541327360 | bytes 6553600 | tf_op jit(solution)/shard_map/oc,cyx->oyx/dot_general | solution.py:48
  80.8 2.7 %fusion.18 = f32[16,256,256]{2,1,0:T(8,128)} fusion(bf16[256,1,256]{0,2,1:T(8,128)(2,1)S(1)} %collective-permute-done.3, bf16[256,16,256]{0,2,1:T(8,128)(2,1)S(1)} %fusion.54, bf16[3,3,256,256]{3,2,1,0:T(8,128)(2,1)S(1)} %copy-done.3), kind=kOutput, calls=%fused_computation.24 | convolution fusion | flops 541327360 | bytes 6553600 | tf_op jit(solution)/shard_map/oc,cyx->oyx/dot_general | solution.py:48
  83.5 13.2 %fusion.72 = bf16[19,16,256]{2,0,1:T(8,128)(2,1)S(1)} fusion(f32[16,256]{1,0:T(8,128)S(1)} %get-tuple-element.22, f32[256]{0:T(256)S(1)} %copy-done.6, bf16[256,18,258]{0,2,1:T(8,128)(2,1)S(1)} %select_maximum_fusion, f32[16,256,256]{2,1,0:T(8,128)} %fusion.18, f32[16,256,256]{2,1,0:T(8,128)} %fusion.26, f32[16,256,256]{2,1,0:T(8,128)} %fusion.28, ...), kind=kOutput, calls=%fused_computation.65 | convolution fusion | flops 589455360 | bytes 35968512 | tf_op jit(solution)/shard_map/kc,cyx->kyx/dot_general | solution.py:95
  96.7 0.7 copy.25
  97.4 0.0 all-gather.2.cloned.1.call-update
  97.4 0.6 fusion.183
  103.7 18.8 %all-gather.2.cloned.1.call-done = bf16[19,128,256]{2,1,0:T(8,128)(2,1)} async-done(((bf16[19,16,256]{2,1,0:T(8,128)(2,1)}), bf16[19,128,256]{2,1,0:T(8,128)(2,1)}) %all-gather.2.cloned.1.call-update) | async-done | bytes 1245200 | tf_op jit(solution)/shard_map/all_gather | solution.py:103
  122.6 1.2 constant_dynamic-slice_fusion.1
  123.7 0.1 copy_bitcast_fusion.6
  123.8 0.7 pad_maximum_fusion
  124.5 3.4 %all-to-all-start = ((bf16[2,19,10,256]{3,1,2,0:T(8,128)(2,1)}), bf16[2,19,10,256]{3,1,2,0:T(8,128)(2,1)S(1)}, u32[]{:S(2)}, u32[]{:S(2)}) async-start(bf16[2,19,10,256]{3,1,2,0:T(8,128)(2,1)} %pad_maximum_fusion), calls=%async_computation | async-start | bytes 491520 | tf_op jit(solution)/shard_map/all_to_all | solution.py:110
  128.0 5.6 %all-to-all-done = bf16[2,19,10,256]{3,1,2,0:T(8,128)(2,1)S(1)} async-done(((bf16[2,19,10,256]{3,1,2,0:T(8,128)(2,1)}), bf16[2,19,10,256]{3,1,2,0:T(8,128)(2,1)S(1)}, u32[]{:S(2)}, u32[]{:S(2)}) %all-to-all-start) | async-done | bytes 194592 | tf_op jit(solution)/shard_map/all_to_all | solution.py:110
  133.6 1.2 fusion.61
  134.9 2.7 %convolution_add_fusion = f32[32,19,1024]{2,0,1:T(8,128)} fusion(f32[32,19,1024]{2,0,1:T(8,128)S(1)} %fusion.61, f32[1024]{0:T(1024)S(1)} %get-tuple-element.35, s32[1024]{0:T(1024)S(1)} %get-tuple-element.38, f32[1024]{0:T(1024)S(1)} %get-tuple-element.36, s32[1024]{0:T(1024)S(1)} %get-tuple-element.37, ...), kind=kOutput, calls=%fused_computation.58 | convolution fusion | flops 114458816 | bytes 5094916 | tf_op jit(solution)/shard_map/iy,cyj->icj/dot_general | solution.py:125
  (24 shorter events, 0.2 us)
Async XLA Ops:
  6.5 76.9 %copy-start = (bf16[19,256]{1,0:T(8,128)(2,1)S(1)}, bf16[19,256]{1,0:T(8,128)(2,1)}, u32[]{:S(2)}) copy-start(bf16[19,256]{1,0:T(8,128)(2,1)} %param.14) | copy-start | bytes 29188
  6.5 116.0 %all-gather.2.cloned.1.call-start = ((), (), s32[]{:S(2)}) async-start(), calls=%async_computation.1 | async-start | bytes 1400832 | tf_op jit(solution)/shard_map/all_gather | solution.py:103
  14.8 6.0 %copy-start.1 = (bf16[1,256,16,256]{3,2,1,0:T(8,128)(2,1)S(1)}, bf16[1,256,16,256]{3,2,1,0:T(8,128)(2,1)}, u32[]{:S(2)}) copy-start(bf16[1,256,16,256]{3,2,1,0:T(8,128)(2,1)} %param.8) | copy-start | bytes 6291460
  16.9 4.0 %copy-start.2 = (bf16[3,3,256,256]{3,2,1,0:T(8,128)(2,1)S(1)}, bf16[3,3,256,256]{3,2,1,0:T(8,128)(2,1)}, u32[]{:S(2)}) copy-start(bf16[3,3,256,256]{3,2,1,0:T(8,128)(2,1)} %param.10) | copy-start | bytes 3538948
  17.0 5.6 %collective-permute-start = (bf16[256,1,256]{0,2,1:T(8,128)(2,1)S(1)}, bf16[256,1,256]{0,2,1:T(8,128)(2,1)S(1)}, u32[]{:S(2)}, u32[]{:S(2)}) collective-permute-start(bf16[256,1,256]{0,2,1:T(8,128)(2,1)S(1)} %get-tuple-element.15), channel_id=1, source_target_pairs={{0,2},{2,4},{4,6},{6,8},{8,10},{10,12},{12,14},{1,3},{3,5},{5,7},{... | collective-permute-start | bytes 393224 | tf_op jit(solution)/shard_map/ppermute | solution.py:14
  19.5 5.4 %collective-permute-start.1 = (bf16[256,1,256]{0,2,1:T(8,128)(2,1)S(1)}, bf16[256,1,256]{0,2,1:T(8,128)(2,1)S(1)}, u32[]{:S(2)}, u32[]{:S(2)}) collective-permute-start(bf16[256,1,256]{0,2,1:T(8,128)(2,1)S(1)} %get-tuple-element.16), channel_id=1, source_target_pairs={{2,0},{4,2},{6,4},{8,6},{10,8},{12,10},{14,12},{3,1},{5,3},{7,5},{... | collective-permute-start | bytes 393224 | tf_op jit(solution)/shard_map/ppermute | solution.py:17
  40.2 2.7 %copy-start.5 = (f32[256]{0:T(256)S(1)}, f32[256]{0:T(256)}, u32[]{:S(2)}) copy-start(f32[256]{0:T(256)} %param.11) | copy-start | bytes 3076
  52.6 10.5 %collective-permute-start.2 = (bf16[256,1,256]{0,2,1:T(8,128)(2,1)S(1)}, bf16[256,1,256]{0,2,1:T(8,128)(2,1)S(1)}, u32[]{:S(2)}, u32[]{:S(2)}) collective-permute-start(bf16[256,1,256]{0,2,1:T(8,128)(2,1)S(1)} %get-tuple-element.13), channel_id=1, source_target_pairs={{0,2},{2,4},{4,6},{6,8},{8,10},{10,12},{12,14},{1,3},{3,5},{5,7},{... | collective-permute-start | bytes 393224 | tf_op jit(solution)/shard_map/ppermute | solution.py:14
  58.1 5.1 %collective-permute-start.3 = (bf16[256,1,256]{0,2,1:T(8,128)(2,1)S(1)}, bf16[256,1,256]{0,2,1:T(8,128)(2,1)S(1)}, u32[]{:S(2)}, u32[]{:S(2)}) collective-permute-start(bf16[256,1,256]{0,2,1:T(8,128)(2,1)S(1)} %get-tuple-element.14), channel_id=1, source_target_pairs={{2,0},{4,2},{6,4},{8,6},{10,8},{12,10},{14,12},{3,1},{5,3},{7,5},{... | collective-permute-start | bytes 393224 | tf_op jit(solution)/shard_map/ppermute | solution.py:17
  63.1 1.3 copy-start.3
  80.8 2.7 %copy-start.6 = (f32[256]{0:T(256)S(1)}, f32[256]{0:T(256)}, u32[]{:S(2)}) copy-start(f32[256]{0:T(256)} %param.13) | copy-start | bytes 3076
  80.8 2.7 %copy-start.7 = (f32[19]{0:T(128)S(1)}, f32[19]{0:T(128)}, u32[]{:S(2)}) copy-start(f32[19]{0:T(128)} %param.15) | copy-start | bytes 232
  83.5 13.9 %copy-start.4 = (s32[2]{0:T(128)S(1)}, s32[2]{0:T(128)}, u32[]{:S(2)}) copy-start(s32[2]{0:T(128)} %param.9) | copy-start | bytes 28
  124.5 9.1 %all-to-all-start = ((bf16[2,19,10,256]{3,1,2,0:T(8,128)(2,1)}), bf16[2,19,10,256]{3,1,2,0:T(8,128)(2,1)S(1)}, u32[]{:S(2)}, u32[]{:S(2)}) async-start(bf16[2,19,10,256]{3,1,2,0:T(8,128)(2,1)} %pad_maximum_fusion), calls=%async_computation | async-start | bytes 491520 | tf_op jit(solution)/shard_map/all_to_all | solution.py:110
Sparse Core Ops, SparseCore 0:
  97.5 24.9 all-gather.1
where the time goes:
time: 145 us; the launch traced here: 144 us
  matrix products  68.2 us (47%)
  waiting for transfers between devices  26.8 us (18%)
  between operations  21.8 us (15%)
  starting transfers between devices  14.2 us (10%)
  local copies, waits for them, and re-layouts  7.31 us (5%)
  other arithmetic  6.15 us (4%)
    dot_general x17, matrix products, convolve(): jnp.einsum('oc,cyx->oyx', weights[row_tap, col_tap], window, preferred_el...  51.1 us
    all_gather x1, waiting for transfers between devices, shards(): gathered = lax.all_gather(logits, 'space', axis=1, tiled=True)  18.8 us
    dot_general x1, matrix products, shards(): jnp.einsum('kc,cyx->kyx', classify, second, preferred_element_type=jnp.fl...  13.2 us
    ppermute x2, starting transfers between devices, with_halo(): lax.ppermute(lax.slice_in_dim(block, block.shape[dim] - width, None, axis...  7.95 us
    all_to_all x1, waiting for transfers between devices, shards(): lax.all_to_all(outgoing, 'member', split_axis=0, concat_axis=0, tiled=True)  5.63 us
    unnamed x17, local copies, waits for them, and re-layouts  4.69 us
    dot_general x2, matrix products, shards(): jnp.einsum('iy,cyj->icj', row_part, widened, preferred_element_type=jnp.f...  3.89 us
    all_to_all x1, starting transfers between devices, shards(): lax.all_to_all(outgoing, 'member', split_axis=0, concat_axis=0, tiled=True)  3.44 us
  transfers between devices with their start and end apart: 6, of which 3 were waited for; matrix products, arithmetic and copies ran while one was open for 4% of the time, Pallas kernels for 0%

commit v1 on v0

--- a/solution.py
+++ b/solution.py
@@ -100,7 +100,16 @@
     own_rows = out_rows // spaces
     part_rows = own_rows // members
     window_rows = (part_rows - 1) // UP + 3
-    gathered = lax.all_gather(logits, "space", axis=1, tiled=True)
+    ways = lax.axis_size("space")
+    up = [(d, (d + 1) % ways) for d in range(ways)]
+    down = [(d, (d - 1) % ways) for d in range(ways)]
+    earlier, later = ([logits], [logits])
+    for _ in range(ways // 2):
+        earlier.append(lax.ppermute(earlier[-1], "space", up))
+    for _ in range((ways - 1) // 2):
+        later.append(lax.ppermute(later[-1], "space", down))
+    line = jnp.concatenate([*earlier[::-1], *later[1:]], axis=1)
+    gathered = jnp.roll(line, (lax.axis_index("space") - ways // 2) * logits.shape[1], axis=1)
     pieces = []
     for target in range(members):
         first_row = place * own_rows + target * part_rows

time: 145 us -> 135 us (0.931)
  between operations: 21.8 us -> 8.35 us
  starting transfers between devices: 14.2 us -> 26.6 us
  waiting for transfers between devices: 26.8 us -> 20 us
  local copies, waits for them, and re-layouts: 7.31 us -> 5.6 us
    all_gather x1 -> x0, waiting for transfers between devices: 18.8 us -> none  [shards(): gathered = lax.all_gather(logits, 'space', axis=1, tiled=True)]
    ppermute x0 -> x7, waiting for transfers between devices: none -> 12.6 us  [the longest x4 7.2 us: shards(): earlier.append(lax.ppermute(earlier[-1], 'space', up))]
    ppermute x0 -> x7, starting transfers between devices: none -> 12.4 us  [the longest x3 11.2 us: shards(): later.append(lax.ppermute(later[-1], 'space', down))]
    unnamed x17 -> x32, local copies, waits for them, and re-layouts: 4.69 us -> 4.92 us
  transfers between devices with their start and end apart: 6 -> 12, of which waited for: 3 -> 8; matrix products, arithmetic and copies ran while one was open for 4% -> 5% of each run, Pallas kernels for 0% -> 0%
where the time goes in v1:
time: 135 us
  matrix products  68.3 us (51%)
  starting transfers between devices  26.6 us (20%)
  waiting for transfers between devices  20 us (15%)
  between operations  8.35 us (6%)
  other arithmetic  6.14 us (5%)
  local copies, waits for them, and re-layouts  5.6 us (4%)
    dot_general x17, matrix products, convolve(): jnp.einsum('oc,cyx->oyx', weights[row_tap, col_tap], window, preferred_el...  51.2 us
    dot_general x1, matrix products, shards(): jnp.einsum('kc,cyx->kyx', classify, second, preferred_element_type=jnp.fl...  13.2 us
    ppermute x3, starting transfers between devices, shards(): later.append(lax.ppermute(later[-1], 'space', down))  11.2 us
    ppermute x2, starting transfers between devices, with_halo(): lax.ppermute(lax.slice_in_dim(block, block.shape[dim] - width, None, axis...  7.97 us
    ppermute x4, waiting for transfers between devices, shards(): earlier.append(lax.ppermute(earlier[-1], 'space', up))  7.2 us
    ppermute x3, waiting for transfers between devices, shards(): later.append(lax.ppermute(later[-1], 'space', down))  5.43 us
    all_to_all x1, waiting for transfers between devices, shards(): lax.all_to_all(outgoing, 'member', split_axis=0, concat_axis=0, tiled=True)  5.05 us
    unnamed x32, local copies, waits for them, and re-layouts  4.92 us
  transfers between devices with their start and end apart: 12, of which 8 were waited for; matrix products, arithmetic and copies ran while one was open for 5% of the time, Pallas kernels for 0%

profile of v1, /device:TPU:0, one launch (start us, length us, event | category | flops | bytes accessed | tf_op | source)
XLA Modules:
  0.0 134.9 jit_solution(17100724385111928481)
XLA Ops:
  0.0 1.3 fusion.174
  4.0 4.3 %copy.9 = bf16[1,256,16,256]{1,3,2,0:T(8,128)(2,1)} copy(bf16[1,256,16,256]{3,2,1,0:T(8,128)(2,1)} %param.8) | data formatting | bytes 4194304 | tf_op args[0]
  8.3 0.1 fusion.151
  8.3 2.1 %bitcast_multiply_fusion = bf16[256,16,256]{0,2,1:T(8,128)(2,1)S(1)} fusion(bf16[1,256,16,256]{1,3,2,0:T(8,128)(2,1)} %copy.9, bf16[16,256]{1,0:T(8,128)(2,1)S(1)} %get-tuple-element.21), kind=kLoop, calls=%fused_computation.54 | loop fusion | flops 1048576 | bytes 4202496 | tf_op jit(solution)/shard_map/mul | solution.py:87
  10.4 0.0 copy-start.2
  10.4 2.5 %collective-permute-start = (bf16[256,1,256]{0,2,1:T(8,128)(2,1)S(1)}, bf16[256,1,256]{0,2,1:T(8,128)(2,1)S(1)}, u32[]{:S(2)}, u32[]{:S(2)}) collective-permute-start(bf16[256,1,256]{0,2,1:T(8,128)(2,1)S(1)} %get-tuple-element.17), channel_id=1, source_target_pairs={{0,2},{2,4},{4,6},{6,8},{8,10},{10,12},{12,14},{1,3},{3,5},{5,7},{... | collective-permute-start | bytes 393224 | tf_op jit(solution)/shard_map/ppermute | solution.py:14
  12.9 1.3 collective-permute-start.1
  14.3 0.1 multiply_bitcast_fusion
  14.4 1.7 %fusion.52 = f32[16,256,256]{2,1,0:T(8,128)S(1)} fusion(bf16[256,16,256]{2,1,0:T(8,128)(2,1)S(1)} %multiply_bitcast_fusion, bf16[3,3,256,256]{3,2,1,0:T(8,128)(2,1)S(1)} %copy-done.2), kind=kOutput, calls=%fused_computation.55 | convolution fusion | flops 536870912 | bytes 6422528 | tf_op jit(solution)/shard_map/oc,cyx->oyx/dot_general | solution.py:48
  16.1 2.3 %collective-permute-done.1 = bf16[256,1,256]{0,2,1:T(8,128)(2,1)S(1)} collective-permute-done((bf16[256,1,256]{0,2,1:T(8,128)(2,1)S(1)}, bf16[256,1,256]{0,2,1:T(8,128)(2,1)S(1)}, u32[]{:S(2)}, u32[]{:S(2)}) %collective-permute-start.1) | collective-permute-done | bytes 131104 | tf_op jit(solution)/shard_map/ppermute | solution.py:17
  18.4 0.8 fusion.5
  19.2 0.7 fusion.40
  20.0 2.8 %fusion.42 = f32[16,256,256]{2,1,0:T(8,128)} fusion(bf16[256,18,258]{0,2,1:T(8,128)(2,1)S(1)} %fusion.5, bf16[3,3,256,256]{3,2,1,0:T(8,128)(2,1)S(1)} %copy-done.2), kind=kOutput, calls=%fused_computation.44 | convolution fusion | flops 536870912 | bytes 6422528 | tf_op jit(solution)/shard_map/oc,cyx->oyx/dot_general | solution.py:48
  22.7 2.7 %fusion.44 = f32[16,256,256]{2,1,0:T(8,128)} fusion(bf16[256,18,258]{0,2,1:T(8,128)(2,1)S(1)} %fusion.5, bf16[3,3,256,256]{3,2,1,0:T(8,128)(2,1)S(1)} %copy-done.2), kind=kOutput, calls=%fused_computation.46 | convolution fusion | flops 536870912 | bytes 6422528 | tf_op jit(solution)/shard_map/oc,cyx->oyx/dot_general | solution.py:48
  25.5 2.7 %fusion.46 = f32[16,256,256]{2,1,0:T(8,128)} fusion(bf16[256,18,258]{0,2,1:T(8,128)(2,1)S(1)} %fusion.5, bf16[3,3,256,256]{3,2,1,0:T(8,128)(2,1)S(1)} %copy-done.2), kind=kOutput, calls=%fused_computation.48 | convolution fusion | flops 536870912 | bytes 6422528 | tf_op jit(solution)/shard_map/oc,cyx->oyx/dot_general | solution.py:48
  28.2 2.7 %fusion.48 = f32[16,256,256]{2,1,0:T(8,128)} fusion(bf16[256,18,258]{0,2,1:T(8,128)(2,1)S(1)} %fusion.5, bf16[3,3,256,256]{3,2,1,0:T(8,128)(2,1)S(1)} %copy-done.2), kind=kOutput, calls=%fused_computation.50 | convolution fusion | flops 536870912 | bytes 6422528 | tf_op jit(solution)/shard_map/oc,cyx->oyx/dot_general | solution.py:48
  30.9 2.8 %fusion.6 = f32[16,256,256]{2,1,0:T(8,128)} fusion(bf16[256,16,256]{0,2,1:T(8,128)(2,1)S(1)} %bitcast_multiply_fusion, bf16[256,1,256]{0,2,1:T(8,128)(2,1)S(1)} %collective-permute-done, bf16[3,3,256,256]{3,2,1,0:T(8,128)(2,1)S(1)} %copy-done.2), kind=kOutput, calls=%fused_computation.12 | convolution fusion | flops 541327360 | bytes 6553600 | tf_op jit(solution)/shard_map/oc,cyx->oyx/dot_general | solution.py:48
  33.6 2.7 %fusion.10 = f32[16,256,256]{2,1,0:T(8,128)} fusion(bf16[256,1,256]{0,2,1:T(8,128)(2,1)S(1)} %collective-permute-done.1, bf16[256,16,256]{0,2,1:T(8,128)(2,1)S(1)} %bitcast_multiply_fusion, bf16[3,3,256,256]{3,2,1,0:T(8,128)(2,1)S(1)} %copy-done.2), kind=kOutput, calls=%fused_computation.16 | convolution fusion | flops 541327360 | bytes 6553600 | tf_op jit(solution)/shard_map/oc,cyx->oyx/dot_general | solution.py:48
  36.3 9.7 %fusion.54 = bf16[256,16,256]{0,2,1:T(8,128)(2,1)S(1)} fusion(f32[16,256]{1,0:T(8,128)S(1)} %get-tuple-element.22, f32[256]{0:T(256)S(1)} %copy-done.5, bf16[256,18,258]{0,2,1:T(8,128)(2,1)S(1)} %fusion.5, f32[16,256,256]{2,1,0:T(8,128)} %fusion.10, f32[16,256,256]{2,1,0:T(8,128)S(1)} %fusion.40, f32[16,256,256]{2,1,0:T(8,128)} %fusion.42, ...), kind=kOutput, calls=%fused_computation.59 | convolution fusion | flops 549453824 | bytes 37897216 | tf_op jit(solution)/shard_map/oc,cyx->oyx/dot_general | solution.py:48
  46.1 5.5 %collective-permute-start.2 = (bf16[256,1,256]{0,2,1:T(8,128)(2,1)S(1)}, bf16[256,1,256]{0,2,1:T(8,128)(2,1)S(1)}, u32[]{:S(2)}, u32[]{:S(2)}) collective-permute-start(bf16[256,1,256]{0,2,1:T(8,128)(2,1)S(1)} %get-tuple-element.15), channel_id=1, source_target_pairs={{0,2},{2,4},{4,6},{6,8},{8,10},{10,12},{12,14},{1,3},{3,5},{5,7},{... | collective-permute-start | bytes 393224 | tf_op jit(solution)/shard_map/ppermute | solution.py:14
  51.6 1.5 %collective-permute-start.3 = (bf16[256,1,256]{0,2,1:T(8,128)(2,1)S(1)}, bf16[256,1,256]{0,2,1:T(8,128)(2,1)S(1)}, u32[]{:S(2)}, u32[]{:S(2)}) collective-permute-start(bf16[256,1,256]{0,2,1:T(8,128)(2,1)S(1)} %get-tuple-element.16), channel_id=1, source_target_pairs={{2,0},{4,2},{6,4},{8,6},{10,8},{12,10},{14,12},{3,1},{5,3},{7,5},{... | collective-permute-start | bytes 393224 | tf_op jit(solution)/shard_map/ppermute | solution.py:17
  53.1 3.6 %fusion.112 = f32[16,256,256]{2,1,0:T(8,128)} fusion(bf16[256,16,256]{0,2,1:T(8,128)(2,1)S(1)} %fusion.54, bf16[3,3,256,256]{3,2,1,0:T(8,128)(2,1)} %param.12), kind=kOutput, calls=%fused_computation.91 | convolution fusion | flops 536870912 | bytes 6422528 | tf_op jit(solution)/shard_map/oc,cyx->oyx/dot_general | solution.py:48
  56.7 0.9 select_maximum_fusion
  57.5 0.4 copy-done.3
  57.9 2.8 %fusion.26 = f32[16,256,256]{2,1,0:T(8,128)} fusion(bf16[256,18,258]{0,2,1:T(8,128)(2,1)S(1)} %select_maximum_fusion, bf16[3,3,256,256]{3,2,1,0:T(8,128)(2,1)S(1)} %copy-done.3), kind=kOutput, calls=%fused_computation.30 | convolution fusion | flops 536870912 | bytes 6422528 | tf_op jit(solution)/shard_map/oc,cyx->oyx/dot_general | solution.py:48
  60.7 2.8 %fusion.28 = f32[16,256,256]{2,1,0:T(8,128)} fusion(bf16[256,18,258]{0,2,1:T(8,128)(2,1)S(1)} %select_maximum_fusion, bf16[3,3,256,256]{3,2,1,0:T(8,128)(2,1)S(1)} %copy-done.3), kind=kOutput, calls=%fused_computation.32 | convolution fusion | flops 536870912 | bytes 6422528 | tf_op jit(solution)/shard_map/oc,cyx->oyx/dot_general | solution.py:48
  63.4 2.7 %fusion.30 = f32[16,256,256]{2,1,0:T(8,128)} fusion(bf16[256,18,258]{0,2,1:T(8,128)(2,1)S(1)} %select_maximum_fusion, bf16[3,3,256,256]{3,2,1,0:T(8,128)(2,1)S(1)} %copy-done.3), kind=kOutput, calls=%fused_computation.34 | convolution fusion | flops 536870912 | bytes 6422528 | tf_op jit(solution)/shard_map/oc,cyx->oyx/dot_general | solution.py:48
  66.1 2.8 %fusion.32 = f32[16,256,256]{2,1,0:T(8,128)} fusion(bf16[256,18,258]{0,2,1:T(8,128)(2,1)S(1)} %select_maximum_fusion, bf16[3,3,256,256]{3,2,1,0:T(8,128)(2,1)S(1)} %copy-done.3), kind=kOutput, calls=%fused_computation.36 | convolution fusion | flops 536870912 | bytes 6422528 | tf_op jit(solution)/shard_map/oc,cyx->oyx/dot_general | solution.py:48
  68.9 2.7 %fusion.34 = f32[16,256,256]{2,1,0:T(8,128)} fusion(bf16[256,18,258]{0,2,1:T(8,128)(2,1)S(1)} %select_maximum_fusion, bf16[3,3,256,256]{3,2,1,0:T(8,128)(2,1)S(1)} %copy-done.3), kind=kOutput, calls=%fused_computation.38 | convolution fusion | flops 536870912 | bytes 6422528 | tf_op jit(solution)/shard_map/oc,cyx->oyx/dot_general | solution.py:48
  71.6 2.7 %fusion.14 = f32[16,256,256]{2,1,0:T(8,128)} fusion(bf16[256,16,256]{0,2,1:T(8,128)(2,1)S(1)} %fusion.54, bf16[256,1,256]{0,2,1:T(8,128)(2,1)S(1)} %collective-permute-done.2, bf16[3,3,256,256]{3,2,1,0:T(8,128)(2,1)S(1)} %copy-done.3), kind=kOutput, calls=%fused_computation.20 | convolution fusion | flops 541327360 | bytes 6553600 | tf_op jit(solution)/shard_map/oc,cyx->oyx/dot_general | solution.py:48
  74.4 2.7 %fusion.18 = f32[16,256,256]{2,1,0:T(8,128)} fusion(bf16[256,1,256]{0,2,1:T(8,128)(2,1)S(1)} %collective-permute-done.3, bf16[256,16,256]{0,2,1:T(8,128)(2,1)S(1)} %fusion.54, bf16[3,3,256,256]{3,2,1,0:T(8,128)(2,1)S(1)} %copy-done.3), kind=kOutput, calls=%fused_computation.24 | convolution fusion | flops 541327360 | bytes 6553600 | tf_op jit(solution)/shard_map/oc,cyx->oyx/dot_general | solution.py:48
  77.1 13.2 %fusion.72 = bf16[19,16,256]{2,0,1:T(8,128)(2,1)S(1)} fusion(f32[16,256]{1,0:T(8,128)S(1)} %get-tuple-element.22, f32[256]{0:T(256)S(1)} %copy-done.6, bf16[256,18,258]{0,2,1:T(8,128)(2,1)S(1)} %select_maximum_fusion, f32[16,256,256]{2,1,0:T(8,128)} %fusion.18, f32[16,256,256]{2,1,0:T(8,128)} %fusion.26, f32[16,256,256]{2,1,0:T(8,128)} %fusion.28, ...), kind=kOutput, calls=%fused_computation.65 | convolution fusion | flops 589455360 | bytes 35968512 | tf_op jit(solution)/shard_map/kc,cyx->kyx/dot_general | solution.py:95
  90.2 1.2 collective-permute-start.4
  91.4 5.8 %collective-permute-done.4 = bf16[19,16,256]{2,0,1:T(8,128)(2,1)S(1)} collective-permute-done((bf16[19,16,256]{2,0,1:T(8,128)(2,1)S(1)}, bf16[19,16,256]{2,0,1:T(8,128)(2,1)S(1)}, u32[]{:S(2)}, u32[]{:S(2)}) %collective-permute-start.4) | collective-permute-done | bytes 155680 | tf_op jit(solution)/shard_map/ppermute | solution.py:108
  97.2 0.6 fusion.186
  100.3 3.6 %collective-permute-start.8 = (bf16[19,16,256]{2,0,1:T(8,128)(2,1)S(1)}, bf16[19,16,256]{2,0,1:T(8,128)(2,1)S(1)}, u32[]{:S(2)}, u32[]{:S(2)}) collective-permute-start(bf16[19,16,256]{2,0,1:T(8,128)(2,1)S(1)} %fusion.72), channel_id=1, source_target_pairs={{0,14},{2,0},{4,2},{6,4},{8,6},{10,8},{12,10},{14,12},{1,15},{3,1}... | collective-permute-start | bytes 466952 | tf_op jit(solution)/shard_map/ppermute | solution.py:110
  103.9 0.2 collective-permute-done.5
  106.8 0.7 collective-permute-done.8
  107.5 3.8 %collective-permute-start.9 = (bf16[19,16,256]{2,0,1:T(8,128)(2,1)S(1)}, bf16[19,16,256]{2,0,1:T(8,128)(2,1)S(1)}, u32[]{:S(2)}, u32[]{:S(2)}) collective-permute-start(bf16[19,16,256]{2,0,1:T(8,128)(2,1)S(1)} %collective-permute-done.8), channel_id=1, source_target_pairs={{0,14},{2,0},{4,2},{6,4},{8,6},{10,8},{12,10},{14,12},{1,15},{3,1}... | collective-permute-start | bytes 466952 | tf_op jit(solution)/shard_map/ppermute | solution.py:110
  111.6 3.0 %collective-permute-done.9 = bf16[19,16,256]{2,0,1:T(8,128)(2,1)S(1)} collective-permute-done((bf16[19,16,256]{2,0,1:T(8,128)(2,1)S(1)}, bf16[19,16,256]{2,0,1:T(8,128)(2,1)S(1)}, u32[]{:S(2)}, u32[]{:S(2)}) %collective-permute-start.9) | collective-permute-done | bytes 155680 | tf_op jit(solution)/shard_map/ppermute | solution.py:110
  114.5 3.8 %collective-permute-start.10 = (bf16[19,16,256]{2,0,1:T(8,128)(2,1)S(1)}, bf16[19,16,256]{2,0,1:T(8,128)(2,1)S(1)}, u32[]{:S(2)}, u32[]{:S(2)}) collective-permute-start(bf16[19,16,256]{2,0,1:T(8,128)(2,1)S(1)} %collective-permute-done.9), channel_id=1, source_target_pairs={{0,14},{2,0},{4,2},{6,4},{8,6},{10,8},{12,10},{14,12},{1,15},{3,1}... | collective-permute-start | bytes 466952 | tf_op jit(solution)/shard_map/ppermute | solution.py:110
  118.3 1.2 collective-permute-done.7
  119.7 1.8 %collective-permute-done.10 = bf16[19,16,256]{2,0,1:T(8,128)(2,1)S(1)} collective-permute-done((bf16[19,16,256]{2,0,1:T(8,128)(2,1)S(1)}, bf16[19,16,256]{2,0,1:T(8,128)(2,1)S(1)}, u32[]{:S(2)}, u32[]{:S(2)}) %collective-permute-start.10) | collective-permute-done | bytes 155680 | tf_op jit(solution)/shard_map/ppermute | solution.py:110
  121.8 0.7 pad_maximum_fusion
  122.5 3.4 %all-to-all-start = ((bf16[2,19,10,256]{3,1,2,0:T(8,128)(2,1)}), bf16[2,19,10,256]{3,1,2,0:T(8,128)(2,1)S(1)}, u32[]{:S(2)}, u32[]{:S(2)}) async-start(bf16[2,19,10,256]{3,1,2,0:T(8,128)(2,1)} %pad_maximum_fusion), calls=%async_computation | async-start | bytes 491520 | tf_op jit(solution)/shard_map/all_to_all | solution.py:119
  126.0 5.0 %all-to-all-done = bf16[2,19,10,256]{3,1,2,0:T(8,128)(2,1)S(1)} async-done(((bf16[2,19,10,256]{3,1,2,0:T(8,128)(2,1)}), bf16[2,19,10,256]{3,1,2,0:T(8,128)(2,1)S(1)}, u32[]{:S(2)}, u32[]{:S(2)}) %all-to-all-start) | async-done | bytes 194592 | tf_op jit(solution)/shard_map/all_to_all | solution.py:119
  131.0 1.2 fusion.61
  132.2 2.7 %convolution_add_fusion = f32[32,19,1024]{2,0,1:T(8,128)} fusion(f32[32,19,1024]{2,0,1:T(8,128)S(1)} %fusion.61, f32[1024]{0:T(1024)S(1)} %get-tuple-element.33, s32[1024]{0:T(1024)S(1)} %get-tuple-element.36, f32[1024]{0:T(1024)S(1)} %get-tuple-element.34, s32[1024]{0:T(1024)S(1)} %get-tuple-element.35, bf16[19,10,256]{2,0,1:T(8,128)(2,1)S(1)} %get-tuple-element.19, ...), kind=kOutput, calls=%fused_computation.58 | convolution fusion | flops 114458816 | bytes 5094916 | tf_op jit(solution)/shard_map/iy,cyj->icj/dot_general | solution.py:134
  (49 shorter events, 0.5 us)
Async XLA Ops:
  0.0 77.0 %copy-start = (bf16[19,256]{1,0:T(8,128)(2,1)S(1)}, bf16[19,256]{1,0:T(8,128)(2,1)}, u32[]{:S(2)}) copy-start(bf16[19,256]{1,0:T(8,128)(2,1)} %param.14) | copy-start | bytes 29188
  8.2 6.0 %copy-start.1 = (bf16[1,256,16,256]{3,2,1,0:T(8,128)(2,1)S(1)}, bf16[1,256,16,256]{3,2,1,0:T(8,128)(2,1)}, u32[]{:S(2)}) copy-start(bf16[1,256,16,256]{3,2,1,0:T(8,128)(2,1)} %param.8) | copy-start | bytes 6291460
  10.4 4.0 %copy-start.2 = (bf16[3,3,256,256]{3,2,1,0:T(8,128)(2,1)S(1)}, bf16[3,3,256,256]{3,2,1,0:T(8,128)(2,1)}, u32[]{:S(2)}) copy-start(bf16[3,3,256,256]{3,2,1,0:T(8,128)(2,1)} %param.10) | copy-start | bytes 3538948
  10.4 5.6 %collective-permute-start = (bf16[256,1,256]{0,2,1:T(8,128)(2,1)S(1)}, bf16[256,1,256]{0,2,1:T(8,128)(2,1)S(1)}, u32[]{:S(2)}, u32[]{:S(2)}) collective-permute-start(bf16[256,1,256]{0,2,1:T(8,128)(2,1)S(1)} %get-tuple-element.17), channel_id=1, source_target_pairs={{0,2},{2,4},{4,6},{6,8},{8,10},{10,12},{12,14},{1,3},{3,5},{5,7},{... | collective-permute-start | bytes 393224 | tf_op jit(solution)/shard_map/ppermute | solution.py:14
  12.9 5.4 %collective-permute-start.1 = (bf16[256,1,256]{0,2,1:T(8,128)(2,1)S(1)}, bf16[256,1,256]{0,2,1:T(8,128)(2,1)S(1)}, u32[]{:S(2)}, u32[]{:S(2)}) collective-permute-start(bf16[256,1,256]{0,2,1:T(8,128)(2,1)S(1)} %get-tuple-element.18), channel_id=1, source_target_pairs={{2,0},{4,2},{6,4},{8,6},{10,8},{12,10},{14,12},{3,1},{5,3},{7,5},{... | collective-permute-start | bytes 393224 | tf_op jit(solution)/shard_map/ppermute | solution.py:17
  33.6 2.7 %copy-start.5 = (f32[256]{0:T(256)S(1)}, f32[256]{0:T(256)}, u32[]{:S(2)}) copy-start(f32[256]{0:T(256)} %param.11) | copy-start | bytes 3076
  46.1 10.6 %collective-permute-start.2 = (bf16[256,1,256]{0,2,1:T(8,128)(2,1)S(1)}, bf16[256,1,256]{0,2,1:T(8,128)(2,1)S(1)}, u32[]{:S(2)}, u32[]{:S(2)}) collective-permute-start(bf16[256,1,256]{0,2,1:T(8,128)(2,1)S(1)} %get-tuple-element.15), channel_id=1, source_target_pairs={{0,2},{2,4},{4,6},{6,8},{8,10},{10,12},{12,14},{1,3},{3,5},{5,7},{... | collective-permute-start | bytes 393224 | tf_op jit(solution)/shard_map/ppermute | solution.py:14
  51.6 5.1 %collective-permute-start.3 = (bf16[256,1,256]{0,2,1:T(8,128)(2,1)S(1)}, bf16[256,1,256]{0,2,1:T(8,128)(2,1)S(1)}, u32[]{:S(2)}, u32[]{:S(2)}) collective-permute-start(bf16[256,1,256]{0,2,1:T(8,128)(2,1)S(1)} %get-tuple-element.16), channel_id=1, source_target_pairs={{2,0},{4,2},{6,4},{8,6},{10,8},{12,10},{14,12},{3,1},{5,3},{7,5},{... | collective-permute-start | bytes 393224 | tf_op jit(solution)/shard_map/ppermute | solution.py:17
  56.7 1.3 copy-start.3
  74.4 2.7 %copy-start.6 = (f32[256]{0:T(256)S(1)}, f32[256]{0:T(256)}, u32[]{:S(2)}) copy-start(f32[256]{0:T(256)} %param.13) | copy-start | bytes 3076
  74.4 2.7 %copy-start.7 = (f32[19]{0:T(128)S(1)}, f32[19]{0:T(128)}, u32[]{:S(2)}) copy-start(f32[19]{0:T(128)} %param.15) | copy-start | bytes 232
  77.1 20.1 %copy-start.4 = (s32[2]{0:T(128)S(1)}, s32[2]{0:T(128)}, u32[]{:S(2)}) copy-start(s32[2]{0:T(128)} %param.9) | copy-start | bytes 28
  90.2 6.9 %collective-permute-start.4 = (bf16[19,16,256]{2,0,1:T(8,128)(2,1)S(1)}, bf16[19,16,256]{2,0,1:T(8,128)(2,1)S(1)}, u32[]{:S(2)}, u32[]{:S(2)}) collective-permute-start(bf16[19,16,256]{2,0,1:T(8,128)(2,1)S(1)} %fusion.72), channel_id=1, source_target_pairs={{0,2},{2,4},{4,6},{6,8},{8,10},{10,12},{12,14},{14,0},{1,3},{3,5},... | collective-permute-start | bytes 466952 | tf_op jit(solution)/shard_map/ppermute | solution.py:108
  97.2 6.9 %collective-permute-start.5 = (bf16[19,16,256]{2,0,1:T(8,128)(2,1)S(1)}, bf16[19,16,256]{2,0,1:T(8,128)(2,1)S(1)}, u32[]{:S(2)}, u32[]{:S(2)}) collective-permute-start(bf16[19,16,256]{2,0,1:T(8,128)(2,1)S(1)} %collective-permute-done.4), channel_id=1, source_target_pairs={{0,2},{2,4},{4,6},{6,8},{8,10},{10,12},{12,14},{14,0},{1,3},{3,5},... | collective-permute-start | bytes 466952 | tf_op jit(solution)/shard_map/ppermute | solution.py:108
  100.3 7.2 %collective-permute-start.8 = (bf16[19,16,256]{2,0,1:T(8,128)(2,1)S(1)}, bf16[19,16,256]{2,0,1:T(8,128)(2,1)S(1)}, u32[]{:S(2)}, u32[]{:S(2)}) collective-permute-start(bf16[19,16,256]{2,0,1:T(8,128)(2,1)S(1)} %fusion.72), channel_id=1, source_target_pairs={{0,14},{2,0},{4,2},{6,4},{8,6},{10,8},{12,10},{14,12},{1,15},{3,1}... | collective-permute-start | bytes 466952 | tf_op jit(solution)/shard_map/ppermute | solution.py:110
  104.1 7.3 %collective-permute-start.6 = (bf16[19,16,256]{2,0,1:T(8,128)(2,1)S(1)}, bf16[19,16,256]{2,0,1:T(8,128)(2,1)S(1)}, u32[]{:S(2)}, u32[]{:S(2)}) collective-permute-start(bf16[19,16,256]{2,0,1:T(8,128)(2,1)S(1)} %collective-permute-done.5), channel_id=1, source_target_pairs={{0,2},{2,4},{4,6},{6,8},{8,10},{10,12},{12,14},{14,0},{1,3},{3,5},... | collective-permute-start | bytes 466952 | tf_op jit(solution)/shard_map/ppermute | solution.py:108
  107.5 7.0 %collective-permute-start.9 = (bf16[19,16,256]{2,0,1:T(8,128)(2,1)S(1)}, bf16[19,16,256]{2,0,1:T(8,128)(2,1)S(1)}, u32[]{:S(2)}, u32[]{:S(2)}) collective-permute-start(bf16[19,16,256]{2,0,1:T(8,128)(2,1)S(1)} %collective-permute-done.8), channel_id=1, source_target_pairs={{0,14},{2,0},{4,2},{6,4},{8,6},{10,8},{12,10},{14,12},{1,15},{3,1}... | collective-permute-start | bytes 466952 | tf_op jit(solution)/shard_map/ppermute | solution.py:110
  111.3 8.2 %collective-permute-start.7 = (bf16[19,16,256]{2,0,1:T(8,128)(2,1)S(1)}, bf16[19,16,256]{2,0,1:T(8,128)(2,1)S(1)}, u32[]{:S(2)}, u32[]{:S(2)}) collective-permute-start(bf16[19,16,256]{2,0,1:T(8,128)(2,1)S(1)} %collective-permute-done.6), channel_id=1, source_target_pairs={{0,2},{2,4},{4,6},{6,8},{8,10},{10,12},{12,14},{14,0},{1,3},{3,5},... | collective-permute-start | bytes 466952 | tf_op jit(solution)/shard_map/ppermute | solution.py:108
  114.5 7.0 %collective-permute-start.10 = (bf16[19,16,256]{2,0,1:T(8,128)(2,1)S(1)}, bf16[19,16,256]{2,0,1:T(8,128)(2,1)S(1)}, u32[]{:S(2)}, u32[]{:S(2)}) collective-permute-start(bf16[19,16,256]{2,0,1:T(8,128)(2,1)S(1)} %collective-permute-done.9), channel_id=1, source_target_pairs={{0,14},{2,0},{4,2},{6,4},{8,6},{10,8},{12,10},{14,12},{1,15},{3,1}... | collective-permute-start | bytes 466952 | tf_op jit(solution)/shard_map/ppermute | solution.py:110
  122.5 8.5 %all-to-all-start = ((bf16[2,19,10,256]{3,1,2,0:T(8,128)(2,1)}), bf16[2,19,10,256]{3,1,2,0:T(8,128)(2,1)S(1)}, u32[]{:S(2)}, u32[]{:S(2)}) async-start(bf16[2,19,10,256]{3,1,2,0:T(8,128)(2,1)} %pad_maximum_fusion), calls=%async_computation | async-start | bytes 491520 | tf_op jit(solution)/shard_map/all_to_all | solution.py:119
